TPU v7x, 256 devices: a whole 4x4x8 slice. The times are simulated.
256 devices in a mesh: expert: 64 (over x, z, core), tensor: 4 (over y).
Axes of the slice: x: 4, y: 4, z: 8, core: 2. Of those that a mesh axis runs over, the one named last changes fastest.
Arguments:
- tokens: bfloat16 [8192, 3584], P('expert'), may hold values from -6 to 6
- cotangent: bfloat16 [8192, 3584], P('expert'), may hold values from -6 to 6
- chosen_experts: int32 [8192, 8], P('expert'), may hold values from 0 to 255, as said below
- chosen_slots: int32 [8192, 8], P('expert'), may hold values from 0 to 127, as said below
- routing_gate_weight: float32 [8192, 8], P('expert'), may hold values from 0.1 to 1
- padded_slot_count: int32 [64, 64], P('expert'), may hold values from 0 to 8, as said below
- w_gate: bfloat16 [64, 3584, 1024], P('expert', None, 'tensor'), may hold values from -0.09375 to 0.09375
- w_up: bfloat16 [64, 3584, 1024], P('expert', None, 'tensor'), may hold values from -0.09375 to 0.09375
- w_down: bfloat16 [64, 1024, 3584], P('expert', 'tensor'), may hold values from -0.1875 to 0.1875
Outputs:
- mixed: bfloat16 [8192, 3584], P('expert', 'tensor')
- token_gradient: bfloat16 [8192, 3584], P('expert', 'tensor')
- gate_gradient: float32 [8192, 8], P('expert')
- grad_w_gate: bfloat16 [64, 3584, 1024], P('expert', None, 'tensor')
- grad_w_up: bfloat16 [64, 3584, 1024], P('expert', None, 'tensor')
- grad_w_down: bfloat16 [64, 1024, 3584], P('expert', 'tensor')
Inputs may be any that keep to these rules, and one draw needn't show every extreme that they name: `chosen_experts`: each token names 8 different experts; only experts under 64 are in flight. `chosen_slots`: within one block of 128 tokens, the routes that name one expert are numbered 0, 1, 2 and so on in order of token and then of route. In every block some expert in flight is named by every token. padded_slot_count[s, e] is the smaller of 8 and the number of routes of block s that name expert e; in every block some expert reaches 8, and some expert in flight is named by no route.
All inputs are finite; a program needn't handle non-finite values.
Results may differ from a plain program's by a relative error of at most 0.015.
Values may be sent and summed in bfloat16 or wider, within the bound.
No kernel may reach another device: no remote copies, remote signals or barrier semaphores. Data moves between devices by JAX's collectives and lax.ppermute only.
A program may use at most 128 MiB of HBM per device.

v0:
```python
import jax
import jax.numpy as jnp
from jax import lax
from jax.sharding import PartitionSpec as P

OWNED = 4


def routing_layout(chosen_expert, chosen_slot, slot_count_row, expert_capacity):
    expert_number = slot_count_row.shape[0]
    one_hot = (
        chosen_expert[:, :, None] == jnp.arange(expert_number, dtype=jnp.int32)[None, None, :]
    ).astype(jnp.int32)
    slot_ceiling = jnp.sum(one_hot * slot_count_row[None, None, :], axis=2)
    slot_alive_mask = (chosen_expert < expert_number) & (chosen_slot < slot_ceiling)
    destination_slot = jnp.where(slot_alive_mask, chosen_expert * expert_capacity + chosen_slot, -1)
    return (slot_alive_mask, destination_slot)


def pack_slots(tok_block, cot_block, block_gates, destination_slot, send_rows):
    select = destination_slot[None, :, :] == jnp.arange(send_rows, dtype=jnp.int32)[:, None, None]
    picked = jnp.sum(select.astype(jnp.int32), axis=2).astype(jnp.bfloat16)
    slot_gate = jnp.sum(jnp.where(select, block_gates[None, :, :], 0.0), axis=(1, 2))
    token_sum = jnp.dot(picked, tok_block, preferred_element_type=jnp.float32).astype(jnp.bfloat16)
    cot_sum = jnp.dot(picked, cot_block, preferred_element_type=jnp.float32)
    return (token_sum, (slot_gate[:, None] * cot_sum).astype(jnp.bfloat16))


def expert_group(expert_rows, expert_cots, gate_weight, up_weight, down_weight):
    pre_gate = jnp.dot(expert_rows, gate_weight, preferred_element_type=jnp.float32)
    pre_up = jnp.dot(expert_rows, up_weight, preferred_element_type=jnp.float32)
    logistic = jax.nn.sigmoid(pre_gate)
    active = pre_gate * logistic
    hidden = (active * pre_up).astype(jnp.bfloat16)
    part_out = jnp.dot(hidden, down_weight, preferred_element_type=jnp.float32)
    grad_hidden = jnp.dot(expert_cots, down_weight.T, preferred_element_type=jnp.float32)
    grad_pre_gate = (grad_hidden * pre_up * logistic * (1.0 + pre_gate * (1.0 - logistic))).astype(
        jnp.bfloat16
    )
    grad_pre_up = (grad_hidden * active).astype(jnp.bfloat16)
    part_back = jnp.dot(grad_pre_gate, gate_weight.T, preferred_element_type=jnp.float32) + jnp.dot(
        grad_pre_up, up_weight.T, preferred_element_type=jnp.float32
    )
    grad_gate_w = jnp.dot(expert_rows.T, grad_pre_gate, preferred_element_type=jnp.float32).astype(
        jnp.bfloat16
    )
    grad_up_w = jnp.dot(expert_rows.T, grad_pre_up, preferred_element_type=jnp.float32).astype(
        jnp.bfloat16
    )
    grad_down_w = jnp.dot(hidden.T, expert_cots, preferred_element_type=jnp.float32).astype(
        jnp.bfloat16
    )
    return (part_out, part_back, (grad_gate_w, grad_up_w, grad_down_w))


def expert_group_t(expert_rows, expert_cots, gate_weight, up_weight, down_weight):
    pre_gate = jnp.dot(expert_rows, gate_weight, preferred_element_type=jnp.float32)
    pre_up = jnp.dot(expert_rows, up_weight, preferred_element_type=jnp.float32)
    logistic = jax.nn.sigmoid(pre_gate)
    active = pre_gate * logistic
    hidden = (active * pre_up).astype(jnp.bfloat16)
    pre_gate, pre_up, logistic, active, hidden = lax.optimization_barrier(
        (pre_gate, pre_up, logistic, active, hidden)
    )
    n_tensor = lax.axis_size("tensor")
    share = gate_weight.shape[0] // n_tensor
    down_parts = down_weight.reshape(down_weight.shape[0], n_tensor, share)
    out_t = jnp.einsum(
        "mh,hkd->kmd", hidden, down_parts, preferred_element_type=jnp.float32
    ).astype(jnp.bfloat16)
    grad_hidden = jnp.dot(expert_cots, down_weight.T, preferred_element_type=jnp.float32)
    grad_pre_gate = (grad_hidden * pre_up * logistic * (1.0 + pre_gate * (1.0 - logistic))).astype(
        jnp.bfloat16
    )
    grad_pre_up = (grad_hidden * active).astype(jnp.bfloat16)
    gate_parts = gate_weight.reshape(n_tensor, share, gate_weight.shape[1])
    up_parts = up_weight.reshape(n_tensor, share, up_weight.shape[1])
    back_t = (
        jnp.einsum("mh,kdh->kmd", grad_pre_gate, gate_parts, preferred_element_type=jnp.float32)
        + jnp.einsum("mh,kdh->kmd", grad_pre_up, up_parts, preferred_element_type=jnp.float32)
    ).astype(jnp.bfloat16)
    grad_gate_w = jnp.dot(expert_rows.T, grad_pre_gate, preferred_element_type=jnp.float32).astype(
        jnp.bfloat16
    )
    grad_up_w = jnp.dot(expert_rows.T, grad_pre_up, preferred_element_type=jnp.float32).astype(
        jnp.bfloat16
    )
    grad_down_w = jnp.dot(hidden.T, expert_cots, preferred_element_type=jnp.float32).astype(
        jnp.bfloat16
    )
    return (out_t, back_t, (grad_gate_w, grad_up_w, grad_down_w))


def local(
    tokens,
    cotangent,
    chosen_experts,
    chosen_slots,
    routing_gate_weight,
    padded_slot_count,
    w_gate,
    w_up,
    w_down,
):
    tok_rows, feature_width = tokens.shape
    per_token = chosen_experts.shape[1]
    expert_number = padded_slot_count.shape[1]
    expert_capacity = 2 * tok_rows * per_token // (OWNED * lax.axis_size("expert"))
    send_rows = expert_number * expert_capacity
    feature_share = feature_width // lax.axis_size("tensor")
    first_col = lax.axis_index("tensor") * feature_share
    slot_alive_mask, destination_slot = routing_layout(
        chosen_experts, chosen_slots, padded_slot_count[0], expert_capacity
    )
    local_tokens = lax.dynamic_slice_in_dim(tokens, first_col, feature_share, 1)
    local_cotangent_bf = lax.dynamic_slice_in_dim(cotangent, first_col, feature_share, 1)
    token_sum, _ = pack_slots(
        local_tokens, local_cotangent_bf[:, :0], routing_gate_weight, destination_slot, send_rows
    )
    _, cot_rows = pack_slots(
        tokens[:, :0], cotangent, routing_gate_weight, destination_slot, send_rows
    )
    rows_q = lax.all_to_all(
        token_sum.reshape(expert_number, expert_capacity, feature_share),
        "expert",
        split_axis=0,
        concat_axis=0,
        tiled=True,
    ).reshape(send_rows, feature_share)
    rows_q, cot_rows = lax.optimization_barrier((rows_q, cot_rows))
    rows_all = lax.all_gather(rows_q, "tensor", axis=1, tiled=True)
    cots_all = lax.all_to_all(
        cot_rows.reshape(expert_number, expert_capacity, feature_width),
        "expert",
        split_axis=0,
        concat_axis=0,
        tiled=True,
    ).reshape(send_rows, feature_width)
    out_t, back_t, grads = expert_group_t(rows_all, cots_all, w_gate[0], w_up[0], w_down[0])
    total_out = lax.psum_scatter(out_t, "tensor", scatter_dimension=0, tiled=True)
    sources = total_out.shape[1] // expert_capacity
    came_out = lax.all_to_all(
        total_out.reshape(sources, expert_capacity, feature_share),
        "expert",
        split_axis=0,
        concat_axis=0,
        tiled=True,
    ).reshape(send_rows, feature_share)
    total_back = lax.psum_scatter(back_t, "tensor", scatter_dimension=0, tiled=True)
    came_back = lax.all_to_all(
        total_back.reshape(sources, expert_capacity, feature_share),
        "expert",
        split_axis=0,
        concat_axis=0,
        tiled=True,
    ).reshape(send_rows, feature_share)
    positions = jnp.maximum(destination_slot, 0).reshape(-1)
    out_rows = (
        jnp.take(came_out, positions, axis=0)
        .reshape(tok_rows, per_token, feature_share)
        .astype(jnp.float32)
    )
    gate_scaling = jnp.where(slot_alive_mask, routing_gate_weight, 0.0)
    mixed = jnp.sum(gate_scaling[:, :, None] * out_rows, axis=1).astype(jnp.bfloat16)
    route_hits = (
        destination_slot[None, :, :] == jnp.arange(send_rows, dtype=jnp.int32)[:, None, None]
    )
    slot_of_token = jnp.sum(route_hits.astype(jnp.int32), axis=2).astype(jnp.bfloat16)
    token_gradient = lax.dot_general(
        slot_of_token, came_back, (((0,), (0,)), ((), ())), preferred_element_type=jnp.float32
    ).astype(jnp.bfloat16)
    local_cotangent = local_cotangent_bf.astype(jnp.float32)
    hidden_totals = jnp.sum(local_cotangent[:, None, :] * out_rows, axis=2)
    gate_gradient = lax.psum(jnp.where(slot_alive_mask, hidden_totals, 0.0), "tensor")
    grad_gate_w, grad_up_w, grad_down_w = grads
    return (
        mixed,
        token_gradient,
        gate_gradient,
        grad_gate_w[None],
        grad_up_w[None],
        grad_down_w[None],
    )


def solution(mesh):
    in_specs = (
        P("expert", None),
        P("expert", None),
        P("expert", None),
        P("expert", None),
        P("expert", None),
        P("expert", None),
        P("expert", None, "tensor"),
        P("expert", None, "tensor"),
        P("expert", "tensor", None),
    )
    out_specs = (
        P("expert", "tensor"),
        P("expert", "tensor"),
        P("expert", None),
        P("expert", None, "tensor"),
        P("expert", None, "tensor"),
        P("expert", "tensor", None),
    )
    return jax.shard_map(local, mesh=mesh, in_specs=in_specs, out_specs=out_specs, check_vma=False)
```

profile of v0, /device:TPU:6, one launch (start us, length us, event | category | flops | bytes accessed | tf_op | source)
XLA Modules:
  0.0 246.5 jit_solution(5502937178036064327)
XLA Ops:
  7.2 0.0 copy-start
  7.2 0.9 select_reduce_fusion.1
  8.1 0.7 broadcast_compare_fusion
  8.9 0.7 convert_reduce_fusion
  9.6 2.3 fusion.14
  11.8 12.2 %all-to-all-start = ((bf16[64,8,896]{2,1,0:T(8,128)(2,1)}), bf16[64,8,896]{2,1,0:T(8,128)(2,1)S(1)}, u32[]{:S(2)}, u32[]{:S(2)}) async-start(bf16[64,8,896]{2,1,0:T(8,128)(2,1)} %fusion.14), calls=%async_computation | async-start | bytes 1835008 | tf_op jit(solution)/shard_map/all_to_all | solution.py:123
  24.0 0.0 all-gather.2.cloned.1.call-start
  24.1 1.0 select_reduce_fusion
  25.1 4.2 %multiply_convert_fusion = bf16[512,3584]{1,0:T(8,128)(2,1)} fusion(bf16[128,3584]{1,0:T(8,128)(2,1)} %param.10, f32[512]{0:T(512)S(1)} %select_reduce_fusion, s32[512,128]{1,0:T(8,128)S(1)} %convert_reduce_fusion), kind=kOutput, calls=%fused_computation.2 | convolution fusion | flops 473497600 | bytes 4851712 | tf_op jit(solution)/shard_map/dot_general | solution.py:25
  29.3 18.9 %all-to-all-done = bf16[64,8,896]{2,1,0:T(8,128)(2,1)S(1)} async-done(((bf16[64,8,896]{2,1,0:T(8,128)(2,1)}), bf16[64,8,896]{2,1,0:T(8,128)(2,1)S(1)}, u32[]{:S(2)}, u32[]{:S(2)}) %all-to-all-start) | async-done | bytes 917536 | tf_op jit(solution)/shard_map/all_to_all | solution.py:123
  48.2 0.9 copy-done.2
  49.1 0.0 all-gather.2.cloned.1.call-update
  49.1 7.9 %all-to-all-start.2 = ((bf16[64,8,3584]{2,1,0:T(8,128)(2,1)}), bf16[64,8,3584]{2,1,0:T(8,128)(2,1)}, u32[]{:S(2)}, u32[]{:S(2)}) async-start(bf16[64,8,3584]{2,1,0:T(8,128)(2,1)} %bitcast.73), calls=%async_computation.3 | async-start | bytes 7340032 | tf_op jit(solution)/shard_map/all_to_all | solution.py:132
  57.1 0.0 reduce-scatter.3.cloned.1.call-start
  57.1 4.3 %reshape_squeeze.9 = bf16[256,4,896]{2,1,0:T(4,128)(2,1)} reshape(bf16[1,256,3584]{2,1,0:T(8,128)(2,1)} %param.17) | data formatting | bytes 3670016 | tf_op jit(solution)/shard_map/reshape;squeeze | solution.py:67
  61.4 32.8 %all-gather.2.cloned.1.call-done = bf16[512,3584]{1,0:T(8,128)(2,1)} async-done(((bf16[512,896]{1,0:T(8,128)(2,1)}), bf16[512,3584]{1,0:T(8,128)(2,1)}) %all-gather.2.cloned.1.call-update) | async-done | bytes 3670032 | tf_op jit(solution)/shard_map/all_gather | solution.py:131
  94.2 3.9 %fusion.11 = f32[512,256]{1,0:T(8,128)S(1)} fusion(bf16[512,3584]{1,0:T(8,128)(2,1)} %all-gather.2.cloned.1.call-done, bf16[1,3584,256]{2,1,0:T(8,128)(2,1)} %param.15), kind=kOutput, calls=%fused_computation.24 | convolution fusion | flops 939524096 | bytes 6029312 | tf_op jit(solution)/shard_map/dot_general | solution.py:57
  98.1 0.0 copy-start.1
  98.1 2.0 multiply_convert_fusion.3
  100.1 0.7 copy-done.4
  100.8 3.0 %convert_bitcast_fusion = bf16[4,512,896]{2,1,0:T(8,128)(2,1)} fusion(bf16[256,4,896]{2,1,0:T(4,128)(2,1)S(1)} %copy-done.1, bf16[512,256]{1,0:T(8,128)(2,1)S(1)} %get-tuple-element.14), kind=kOutput, calls=%fused_computation.16 | convolution fusion | flops 941359104 | bytes 5767168 | tf_op jit(solution)/shard_map/mh,hkd->kmd/dot_general | solution.py:68
  103.9 0.0 reduce-scatter.3.cloned.1.call-update
  103.9 0.0 reduce-scatter.5.cloned.1.call-start
  104.0 35.7 %all-to-all-done.2 = bf16[64,8,3584]{2,1,0:T(8,128)(2,1)} async-done(((bf16[64,8,3584]{2,1,0:T(8,128)(2,1)}), bf16[64,8,3584]{2,1,0:T(8,128)(2,1)}, u32[]{:S(2)}, u32[]{:S(2)}) %all-to-all-start.2) | async-done | bytes 3670048 | tf_op jit(solution)/shard_map/all_to_all | solution.py:132
  139.7 4.2 %multiply_convert_fusion.1 = (bf16[512,256]{1,0:T(8,128)(2,1)S(1)}, bf16[512,256]{1,0:T(8,128)(2,1)S(1)}) fusion(f32[512,256]{1,0:T(8,128)S(1)} %get-tuple-element.19, f32[512,256]{1,0:T(8,128)S(1)} %fusion.11, f32[512,256]{1,0:T(8,128)} %get-tuple-element.17, f32[512,256]{1,0:T(8,128)} %get-tuple-element.16, bf16[1,256,3584]{2,1,0:T(8,128)(2,1)} %param.17, ...), kind=kOutput, calls=%fused_computation.31 | convolution fusion | flops 940703744 | bytes 8126464 | tf_op jit(solution)/shard_map/dot_general | solution.py:71
  143.9 1.1 fusion.17
  145.0 3.1 %fusion.3 = bf16[4,512,896]{2,1,0:T(8,128)(2,1)} fusion(f32[512,4,896]{2,0,1:T(8,128)S(1)} %fusion.17, bf16[4,896,256]{2,1,0:T(8,128)(2,1)S(1)} %bitcast.71, bf16[512,256]{1,0:T(8,128)(2,1)S(1)} %get-tuple-element.29), kind=kOutput, calls=%fused_computation.9 | convolution fusion | flops 943194112 | bytes 13107200 | tf_op jit(solution)/shard_map/mh,kdh->kmd/dot_general | solution.py:80
  148.2 0.0 reduce-scatter.5.cloned.1.call-update
  148.2 1.3 reduce-scatter.3.cloned.1.call-done
  149.5 10.7 %all-to-all-start.1 = ((bf16[64,8,896]{2,1,0:T(8,128)(2,1)}), bf16[64,8,896]{2,1,0:T(8,128)(2,1)S(1)}, u32[]{:S(2)}, u32[]{:S(2)}) async-start(bf16[64,8,896]{2,1,0:T(8,128)(2,1)} %bitcast.77), calls=%async_computation.2 | async-start | bytes 1835008 | tf_op jit(solution)/shard_map/all_to_all | solution.py:142
  160.2 0.1 copy.34
  160.3 0.1 broadcast_in_dim.64
  160.5 0.1 copy.36
  160.6 0.1 reshape.104
  160.7 1.0 dynamic-slice_convert_fusion
  161.7 35.3 %reduce-scatter.5.cloned.1.call-done = bf16[1,512,896]{2,1,0:T(8,128)(2,1)} async-done(((bf16[4,512,896]{2,1,0:T(8,128)(2,1)}), bf16[1,512,896]{2,1,0:T(8,128)(2,1)}) %reduce-scatter.5.cloned.1.call-update) | async-done | bytes 917520 | tf_op jit(solution)/shard_map/reduce_scatter | solution.py:149
  197.0 10.9 %all-to-all-start.3 = ((bf16[64,8,896]{2,1,0:T(8,128)(2,1)}), bf16[64,8,896]{2,1,0:T(8,128)(2,1)}, u32[]{:S(2)}, u32[]{:S(2)}) async-start(bf16[64,8,896]{2,1,0:T(8,128)(2,1)} %bitcast.76), calls=%async_computation.5 | async-start | bytes 1835008 | tf_op jit(solution)/shard_map/all_to_all | solution.py:150
  207.9 0.0 copy-start.8
  207.9 4.6 %fusion.2 = bf16[1,256,3584]{2,1,0:T(8,128)(2,1)} fusion(bf16[512,256]{1,0:T(8,128)(2,1)} %copy-done.4, bf16[64,8,3584]{2,1,0:T(8,128)(2,1)} %all-to-all-done.2), kind=kOutput, calls=%fused_computation.8 | convolution fusion | flops 940441600 | bytes 5767168 | tf_op jit(solution)/shard_map/dot_general | solution.py:88
  212.5 2.4 fusion.1
  214.9 2.4 fusion
  217.3 5.3 %gather_fusion = bf16[1024,896]{1,0:T(8,128)(2,1)} fusion(bf16[512,896]{1,0:T(8,128)(2,1)S(1)} %bitcast.72, s32[1024]{0:T(1024)S(1)} %broadcast_clamp_fusion), kind=kCustom, calls=%fused_computation | custom fusion | bytes 3674112 | tf_op jit(solution)/shard_map/jit(_take)/gather | solution.py:159
  222.6 2.2 fusion.4
  224.8 0.1 reduce_sum.60
  225.0 0.1 copy.33
  225.1 9.2 %psum.7 = f32[128,8]{0,1:T(8,128)} all-reduce(f32[128,8]{0,1:T(8,128)S(1)} %get-tuple-element.34), channel_id=1, replica_groups=mesh['expert'=64,'tensor'=4] {'tensor'}, use_global_device_ids=true, to_apply=%region_7.8 | all-reduce | flops 1024 | bytes 8192 | tf_op jit(solution)/shard_map/psum | solution.py:174
  234.3 3.5 %multiply_reduce_fusion = bf16[128,896]{1,0:T(8,128)(2,1)} fusion(bf16[1024,896]{1,0:T(8,128)(2,1)} %gather_fusion, f32[128,8]{1,0:T(8,128)S(1)} %copy.33, pred[128,8]{1,0:T(8,128)(4,1)S(1)} %copy.34), kind=kLoop, calls=%fused_computation.15 | loop fusion | flops 3555328 | bytes 2069504 | tf_op jit(solution)/shard_map/reduce_sum | solution.py:164
  237.8 2.2 convolution_convert_fusion.4
  (26 shorter events, 0.1 us)
Async XLA Ops:
  7.2 90.9 %copy-start = (bf16[1,3584,256]{2,1,0:T(8,128)(2,1)S(1)}, bf16[1,3584,256]{2,1,0:T(8,128)(2,1)}, u32[]{:S(2)}) copy-start(bf16[1,3584,256]{2,1,0:T(8,128)(2,1)} %param.16) | copy-start | bytes 5505028
  7.2 16.9 %copy-start.9 = (f32[128,8]{0,1:T(8,128)S(1)}, f32[128,8]{0,1:T(8,128)}, u32[]{:S(2)}) copy-start(f32[128,8]{0,1:T(8,128)} %param.13) | copy-start | bytes 12292
  11.8 36.3 %all-to-all-start = ((bf16[64,8,896]{2,1,0:T(8,128)(2,1)}), bf16[64,8,896]{2,1,0:T(8,128)(2,1)S(1)}, u32[]{:S(2)}, u32[]{:S(2)}) async-start(bf16[64,8,896]{2,1,0:T(8,128)(2,1)} %fusion.14), calls=%async_computation | async-start | bytes 1835008 | tf_op jit(solution)/shard_map/all_to_all | solution.py:123
  24.0 70.2 %all-gather.2.cloned.1.call-start = ((), (), s32[]{:S(2)}) async-start(), calls=%async_computation.6 | async-start | bytes 4587520 | tf_op jit(solution)/shard_map/all_gather | solution.py:131
  48.2 0.9 copy-start.2
  49.1 90.5 %all-to-all-start.2 = ((bf16[64,8,3584]{2,1,0:T(8,128)(2,1)}), bf16[64,8,3584]{2,1,0:T(8,128)(2,1)}, u32[]{:S(2)}, u32[]{:S(2)}) async-start(bf16[64,8,3584]{2,1,0:T(8,128)(2,1)} %bitcast.73), calls=%async_computation.3 | async-start | bytes 7340032 | tf_op jit(solution)/shard_map/all_to_all | solution.py:132
  57.1 92.4 %reduce-scatter.3.cloned.1.call-start = ((), (), s32[]{:S(2)}) async-start(), calls=%async_computation.7 | async-start | bytes 4587520 | tf_op jit(solution)/shard_map/reduce_scatter | solution.py:140
  94.2 3.9 %copy-start.10 = (bf16[512,3584]{1,0:T(8,128)(2,1)S(1)}, bf16[512,3584]{1,0:T(8,128)(2,1)}, u32[]{:S(2)}) copy-start(bf16[512,3584]{1,0:T(8,128)(2,1)} %all-gather.2.cloned.1.call-done) | copy-start | bytes 11010052
  98.1 2.7 %copy-start.1 = (bf16[256,4,896]{2,1,0:T(4,128)(2,1)S(1)}, bf16[256,4,896]{2,1,0:T(4,128)(2,1)}, u32[]{:S(2)}) copy-start(bf16[256,4,896]{2,1,0:T(4,128)(2,1)} %reshape_squeeze.9) | copy-start | bytes 5505028
  100.1 0.7 copy-start.4
  103.9 93.0 %reduce-scatter.5.cloned.1.call-start = ((), (), s32[]{:S(2)}) async-start(), calls=%async_computation.8 | async-start | bytes 4587520 | tf_op jit(solution)/shard_map/reduce_scatter | solution.py:149
  139.7 4.2 %copy-start.3 = (bf16[1,3584,256]{2,1,0:T(8,128)(2,1)S(1)}, bf16[1,3584,256]{2,1,0:T(8,128)(2,1)}, u32[]{:S(2)}) copy-start(bf16[1,3584,256]{2,1,0:T(8,128)(2,1)} %param.15) | copy-start | bytes 5505028
  143.8 1.2 copy-start.5
  143.8 1.2 copy-start.7
  149.5 47.5 %all-to-all-start.1 = ((bf16[64,8,896]{2,1,0:T(8,128)(2,1)}), bf16[64,8,896]{2,1,0:T(8,128)(2,1)S(1)}, u32[]{:S(2)}, u32[]{:S(2)}) async-start(bf16[64,8,896]{2,1,0:T(8,128)(2,1)} %bitcast.77), calls=%async_computation.2 | async-start | bytes 1835008 | tf_op jit(solution)/shard_map/all_to_all | solution.py:142
  197.0 40.8 %all-to-all-start.3 = ((bf16[64,8,896]{2,1,0:T(8,128)(2,1)}), bf16[64,8,896]{2,1,0:T(8,128)(2,1)}, u32[]{:S(2)}, u32[]{:S(2)}) async-start(bf16[64,8,896]{2,1,0:T(8,128)(2,1)} %bitcast.76), calls=%async_computation.5 | async-start | bytes 1835008 | tf_op jit(solution)/shard_map/all_to_all | solution.py:150
  207.9 4.7 %copy-start.8 = (bf16[512,256]{1,0:T(8,128)(2,1)S(1)}, bf16[512,256]{1,0:T(8,128)(2,1)}, u32[]{:S(2)}) copy-start(bf16[512,256]{1,0:T(8,128)(2,1)} %copy-done.7) | copy-start | bytes 786436
  207.9 4.7 %copy-start.11 = (bf16[512,3584]{1,0:T(8,128)(2,1)S(1)}, bf16[512,3584]{1,0:T(8,128)(2,1)}, u32[]{:S(2)}) copy-start(bf16[512,3584]{1,0:T(8,128)(2,1)} %all-gather.2.cloned.1.call-done) | copy-start | bytes 11010052
  212.5 2.4 copy-start.6
Sparse Core Ops, SparseCore 0:
  49.3 44.9 all-gather.1
  104.0 45.4 reduce-scatter.2
  152.0 44.8 reduce-scatter.4
where the time goes:
time: 247 us
  waiting for transfers between devices  124 us (50%)
  starting transfers between devices  41.9 us (17%)
  matrix products  35.5 us (14%)
  between operations  14 us (6%)
  local copies, waits for them, and re-layouts  11.9 us (5%)
  other arithmetic  10.2 us (4%)
  blocking collectives  9.16 us (4%)
    all_to_all x1, waiting for transfers between devices, local(): lax.all_to_all(cot_rows.reshape(expert_number, expert_capacity, feature_w...  35.7 us
    reduce_scatter x1, waiting for transfers between devices, local(): lax.psum_scatter(back_t, 'tensor', scatter_dimension=0, tiled=True)  35.3 us
    all_gather x1, waiting for transfers between devices, local(): rows_all = lax.all_gather(rows_q, 'tensor', axis=1, tiled=True)  32.8 us
    all_to_all x1, waiting for transfers between devices, local(): lax.all_to_all(token_sum.reshape(expert_number, expert_capacity, feature_...  18.9 us
    all_to_all x1, starting transfers between devices, local(): lax.all_to_all(token_sum.reshape(expert_number, expert_capacity, feature_...  12.2 us
    all_to_all x1, starting transfers between devices, local(): lax.all_to_all(total_back.reshape(sources, expert_capacity, feature_share...  10.9 us
    all_to_all x1, starting transfers between devices, local(): lax.all_to_all(total_out.reshape(sources, expert_capacity, feature_share)...  10.7 us
    psum x1, blocking collectives, local(): lax.psum(jnp.where(slot_alive_mask, hidden_totals, 0.0), 'tensor')  9.16 us
  transfers between devices with their start and end apart: 7, of which 5 were waited for; matrix products, arithmetic and copies ran while one was open for 20% of the time, Pallas kernels for 0%

commit v1 on v0

--- a/solution.py
+++ b/solution.py
@@ -1,9 +1,44 @@
+import functools
 import jax
 import jax.numpy as jnp
 from jax import lax
 from jax.sharding import PartitionSpec as P
+from jax.lax import axis_index, axis_size, ppermute
 
 OWNED = 4
+
+
+def _number_thing(message, dev_axis):
+    aux = axis_size(dev_axis)
+    even = axis_index(dev_axis)
+    local_next, current_value, outer = (aux, even, message.shape[1])
+    gallery = []
+    for dev_i, j in enumerate(message.shape):
+        gallery.append(j * local_next if dev_i == 1 else j)
+    piece_now = lax.dynamic_update_slice_in_dim(
+        jnp.zeros(gallery, message.dtype), message, current_value * outer, axis=1
+    )
+    f_next = mixed_arr = message
+    for m in tuple(range(1, local_next // 2 + 1)):
+        queue = []
+        for dev_i in tuple(range(local_next)):
+            queue.append((dev_i, (dev_i + 1) % local_next))
+        f_next = ppermute(f_next, dev_axis, queue)
+        piece_now = lax.dynamic_update_slice_in_dim(
+            piece_now, f_next, (current_value - m) % local_next * outer, axis=1
+        )
+        if 2 * m < local_next:
+            leaves = []
+            for dev_i in [*range(local_next)]:
+                leaves.append((dev_i, (dev_i - 1) % local_next))
+            mixed_arr = ppermute(mixed_arr, dev_axis, leaves)
+            piece_now = lax.dynamic_update_slice_in_dim(
+                piece_now, mixed_arr, (current_value + m) % local_next * outer, axis=1
+            )
+    return piece_now
+
+
+islands_resolve = functools.partial(_number_thing, dev_axis="tensor")
 
 
 def routing_layout(chosen_expert, chosen_slot, slot_count_row, expert_capacity):
@@ -128,7 +163,7 @@
         tiled=True,
     ).reshape(send_rows, feature_share)
     rows_q, cot_rows = lax.optimization_barrier((rows_q, cot_rows))
-    rows_all = lax.all_gather(rows_q, "tensor", axis=1, tiled=True)
+    rows_all = islands_resolve(rows_q)
     cots_all = lax.all_to_all(
         cot_rows.reshape(expert_number, expert_capacity, feature_width),
         "expert",

time: 247 us -> 270 us (1.093)
  waiting for transfers between devices: 124 us -> 144 us
  local copies, waits for them, and re-layouts: 11.9 us -> 15.3 us
  matrix products: 35.5 us -> 32.4 us
    all_gather x1 -> x0, waiting for transfers between devices: 32.8 us -> none  [local(): rows_all = lax.all_gather(rows_q, 'tensor', axis=1, tiled=True)]
    ppermute x0 -> x3, waiting for transfers between devices: none -> 29.6 us  [the longest x2 29.6 us: _number_thing(): f_next = ppermute(f_next, dev_axis, queue)]
    all_to_all x1, waiting for transfers between devices: 35.7 us -> 62 us  [local(): lax.all_to_all(cot_rows.reshape(expert_number, expert_capacity, feature_w...]
    reduce_scatter x1, waiting for transfers between devices: 35.3 us -> 11.6 us  [local(): lax.psum_scatter(back_t, 'tensor', scatter_dimension=0, tiled=True)]
    all_to_all x1, waiting for transfers between devices: 0.01 us -> 22.7 us  [local(): lax.all_to_all(total_out.reshape(sources, expert_capacity, feature_share)...]
    dynamic_update_slice x0 -> x4, local copies, waits for them, and re-layouts: none -> 4.18 us  [the longest x2 2.73 us: _number_thing(): lax.dynamic_update_slice_in_dim(piece_now, f_next, (current_value - m) %...]
    ppermute x0 -> x3, starting transfers between devices: none -> 3.67 us  [the longest x2 2.01 us: _number_thing(): f_next = ppermute(f_next, dev_axis, queue)]
    all_to_all x1, starting transfers between devices: 10.7 us -> 7.8 us  [local(): lax.all_to_all(total_out.reshape(sources, expert_capacity, feature_share)...]
  transfers between devices with their start and end apart: 7 -> 9, of which waited for: 5 -> 6; matrix products, arithmetic and copies ran while one was open for 20% -> 19% of each run, Pallas kernels for 0% -> 0%
where the time goes in v1:
time: 270 us; the launch traced here: 269 us
  waiting for transfers between devices  144 us (53%)
  starting transfers between devices  42.3 us (16%)
  matrix products  32.4 us (12%)
  local copies, waits for them, and re-layouts  15.3 us (6%)
  between operations  14.3 us (5%)
  other arithmetic  11.1 us (4%)
  blocking collectives  9.17 us (3%)
    all_to_all x1, waiting for transfers between devices, local(): lax.all_to_all(cot_rows.reshape(expert_number, expert_capacity, feature_w...  62 us
    ppermute x2, waiting for transfers between devices, _number_thing(): f_next = ppermute(f_next, dev_axis, queue)  29.6 us
    all_to_all x1, waiting for transfers between devices, local(): lax.all_to_all(total_out.reshape(sources, expert_capacity, feature_share)...  22.7 us
    all_to_all x1, waiting for transfers between devices, local(): lax.all_to_all(token_sum.reshape(expert_number, expert_capacity, feature_...  18.2 us
    all_to_all x1, starting transfers between devices, local(): lax.all_to_all(token_sum.reshape(expert_number, expert_capacity, feature_...  12.2 us
    reduce_scatter x1, waiting for transfers between devices, local(): lax.psum_scatter(back_t, 'tensor', scatter_dimension=0, tiled=True)  11.6 us
    all_to_all x1, starting transfers between devices, local(): lax.all_to_all(total_back.reshape(sources, expert_capacity, feature_share...  10.9 us
    psum x1, blocking collectives, local(): lax.psum(jnp.where(slot_alive_mask, hidden_totals, 0.0), 'tensor')  9.17 us
  transfers between devices with their start and end apart: 9, of which 6 were waited for; matrix products, arithmetic and copies ran while one was open for 19% of the time, Pallas kernels for 0%

profile of v1, /device:TPU:6, one launch (start us, length us, event | category | flops | bytes accessed | tf_op | source)
XLA Modules:
  0.0 268.8 jit_solution(9174965412390799929)
XLA Ops:
  7.2 0.9 select_reduce_fusion.1
  8.1 0.7 broadcast_compare_fusion
  8.8 0.7 convert_reduce_fusion
  9.6 2.3 fusion.14
  11.8 12.2 %all-to-all-start = ((bf16[64,8,896]{2,1,0:T(8,128)(2,1)}), bf16[64,8,896]{2,1,0:T(8,128)(2,1)S(1)}, u32[]{:S(2)}, u32[]{:S(2)}) async-start(bf16[64,8,896]{2,1,0:T(8,128)(2,1)} %fusion.14), calls=%async_computation | async-start | bytes 1835008 | tf_op jit(solution)/shard_map/all_to_all | solution.py:158
  24.0 1.7 select_reduce_fusion
  25.7 4.2 %multiply_convert_fusion = bf16[512,3584]{1,0:T(8,128)(2,1)} fusion(bf16[128,3584]{1,0:T(8,128)(2,1)} %param.10, f32[512]{0:T(512)S(1)} %select_reduce_fusion, s32[512,128]{1,0:T(8,128)S(1)} %convert_reduce_fusion), kind=kOutput, calls=%fused_computation.2 | convolution fusion | flops 473497600 | bytes 4851712 | tf_op jit(solution)/shard_map/dot_general | solution.py:60
  29.9 18.2 %all-to-all-done = bf16[64,8,896]{2,1,0:T(8,128)(2,1)S(1)} async-done(((bf16[64,8,896]{2,1,0:T(8,128)(2,1)}), bf16[64,8,896]{2,1,0:T(8,128)(2,1)S(1)}, u32[]{:S(2)}, u32[]{:S(2)}) %all-to-all-start) | async-done | bytes 917536 | tf_op jit(solution)/shard_map/all_to_all | solution.py:158
  48.2 1.6 collective-permute-start
  49.7 1.7 collective-permute-start.1
  51.4 20.7 %collective-permute-done = bf16[512,896]{1,0:T(8,128)(2,1)} collective-permute-done((bf16[512,896]{1,0:T(8,128)(2,1)S(1)}, bf16[512,896]{1,0:T(8,128)(2,1)}, u32[]{:S(2)}, u32[]{:S(2)}) %collective-permute-start) | collective-permute-done | bytes 917536 | tf_op jit(solution)/shard_map/ppermute | solution.py:26
  72.1 0.4 collective-permute-start.2
  72.5 4.2 %reshape_squeeze.9 = bf16[256,4,896]{2,1,0:T(4,128)(2,1)} reshape(bf16[1,256,3584]{2,1,0:T(8,128)(2,1)} %param.17) | data formatting | bytes 3670016 | tf_op jit(solution)/shard_map/reshape;squeeze | solution.py:102
  76.7 7.5 %all-to-all-start.2 = ((bf16[64,8,3584]{2,1,0:T(8,128)(2,1)}), bf16[64,8,3584]{2,1,0:T(8,128)(2,1)}, u32[]{:S(2)}, u32[]{:S(2)}) async-start(bf16[64,8,3584]{2,1,0:T(8,128)(2,1)} %bitcast.69), calls=%async_computation.3 | async-start | bytes 7340032 | tf_op jit(solution)/shard_map/all_to_all | solution.py:167
  84.2 0.2 broadcast_in_dim.64
  84.5 0.1 constant_dynamic-update-slice_fusion.3
  84.6 1.4 constant_dynamic-update-slice_fusion.2
  86.1 1.3 constant_dynamic-update-slice_fusion.1
  87.4 8.9 %collective-permute-done.2 = bf16[512,896]{1,0:T(8,128)(2,1)} collective-permute-done((bf16[512,896]{1,0:T(8,128)(2,1)}, bf16[512,896]{1,0:T(8,128)(2,1)}, u32[]{:S(2)}, u32[]{:S(2)}) %collective-permute-start.2) | collective-permute-done | bytes 917536 | tf_op jit(solution)/shard_map/ppermute | solution.py:26
  96.3 1.3 constant_dynamic-update-slice_fusion
  97.6 1.1 fusion.11
  98.8 2.0 multiply_convert_fusion.3
  100.8 0.7 copy-done.6
  101.5 3.0 %convert_bitcast_fusion = bf16[4,512,896]{2,1,0:T(8,128)(2,1)} fusion(bf16[256,4,896]{2,1,0:T(4,128)(2,1)S(1)} %copy-done.1, bf16[512,256]{1,0:T(8,128)(2,1)S(1)} %get-tuple-element.14), kind=kOutput, calls=%fused_computation.16 | convolution fusion | flops 941359104 | bytes 5767168 | tf_op jit(solution)/shard_map/mh,hkd->kmd/dot_general | solution.py:103
  104.6 0.2 reduce-scatter.5.cloned.1.call-start
  104.8 62.0 %all-to-all-done.2 = bf16[64,8,3584]{2,1,0:T(8,128)(2,1)} async-done(((bf16[64,8,3584]{2,1,0:T(8,128)(2,1)}), bf16[64,8,3584]{2,1,0:T(8,128)(2,1)}, u32[]{:S(2)}, u32[]{:S(2)}) %all-to-all-start.2) | async-done | bytes 3670048 | tf_op jit(solution)/shard_map/all_to_all | solution.py:167
  166.8 3.9 %fusion.6 = f32[512,256]{1,0:T(8,128)S(1)} fusion(bf16[64,8,3584]{2,1,0:T(8,128)(2,1)} %all-to-all-done.2, bf16[1,256,3584]{2,1,0:T(8,128)(2,1)} %param.17), kind=kOutput, calls=%fused_computation.13 | convolution fusion | flops 939524096 | bytes 6029312 | tf_op jit(solution)/shard_map/dot_general | solution.py:106
  170.7 0.3 multiply_convert_fusion.1
  171.0 1.2 fusion.17
  172.2 3.1 %fusion.3 = bf16[4,512,896]{2,1,0:T(8,128)(2,1)} fusion(f32[512,4,896]{2,0,1:T(8,128)S(1)} %fusion.17, bf16[4,896,256]{2,1,0:T(8,128)(2,1)S(1)} %bitcast.67, bf16[512,256]{1,0:T(8,128)(2,1)S(1)} %get-tuple-element.29), kind=kOutput, calls=%fused_computation.9 | convolution fusion | flops 943194112 | bytes 13107200 | tf_op jit(solution)/shard_map/mh,kdh->kmd/dot_general | solution.py:115
  175.4 7.8 %all-to-all-start.1 = ((bf16[64,8,896]{2,1,0:T(8,128)(2,1)}), bf16[64,8,896]{2,1,0:T(8,128)(2,1)S(1)}, u32[]{:S(2)}, u32[]{:S(2)}) async-start(bf16[64,8,896]{2,1,0:T(8,128)(2,1)} %bitcast.75), calls=%async_computation.2 | async-start | bytes 1835008 | tf_op jit(solution)/shard_map/all_to_all | solution.py:177
  183.2 0.1 copy.34
  183.3 0.1 broadcast_in_dim.68
  183.4 0.1 copy.36
  183.5 0.1 reshape.104
  183.6 1.0 dynamic-slice_convert_fusion
  184.6 22.7 %all-to-all-done.1 = bf16[64,8,896]{2,1,0:T(8,128)(2,1)S(1)} async-done(((bf16[64,8,896]{2,1,0:T(8,128)(2,1)}), bf16[64,8,896]{2,1,0:T(8,128)(2,1)S(1)}, u32[]{:S(2)}, u32[]{:S(2)}) %all-to-all-start.1) | async-done | bytes 917536 | tf_op jit(solution)/shard_map/all_to_all | solution.py:177
  207.3 11.6 %reduce-scatter.5.cloned.1.call-done = bf16[1,512,896]{2,1,0:T(8,128)(2,1)} async-done(((bf16[4,512,896]{2,1,0:T(8,128)(2,1)}), bf16[1,512,896]{2,1,0:T(8,128)(2,1)}) %reduce-scatter.5.cloned.1.call-update) | async-done | bytes 917520 | tf_op jit(solution)/shard_map/reduce_scatter | solution.py:184
  218.9 10.9 %all-to-all-start.3 = ((bf16[64,8,896]{2,1,0:T(8,128)(2,1)}), bf16[64,8,896]{2,1,0:T(8,128)(2,1)}, u32[]{:S(2)}, u32[]{:S(2)}) async-start(bf16[64,8,896]{2,1,0:T(8,128)(2,1)} %bitcast.74), calls=%async_computation.5 | async-start | bytes 1835008 | tf_op jit(solution)/shard_map/all_to_all | solution.py:185
  229.8 4.6 %fusion.2 = bf16[1,256,3584]{2,1,0:T(8,128)(2,1)} fusion(bf16[512,256]{1,0:T(8,128)(2,1)} %copy-done.6, bf16[64,8,3584]{2,1,0:T(8,128)(2,1)} %all-to-all-done.2), kind=kOutput, calls=%fused_computation.8 | convolution fusion | flops 940441600 | bytes 5767168 | tf_op jit(solution)/shard_map/dot_general | solution.py:123
  234.5 2.4 fusion.1
  236.9 2.4 fusion
  239.3 5.3 %gather_fusion = bf16[1024,896]{1,0:T(8,128)(2,1)} fusion(bf16[512,896]{1,0:T(8,128)(2,1)S(1)} %bitcast.68, s32[1024]{0:T(1024)S(1)} %broadcast_clamp_fusion), kind=kCustom, calls=%fused_computation | custom fusion | bytes 3674112 | tf_op jit(solution)/shard_map/jit(_take)/gather | solution.py:194
  244.6 2.2 fusion.4
  247.0 0.1 copy.33
  247.1 9.2 %psum.7 = f32[128,8]{0,1:T(8,128)} all-reduce(f32[128,8]{0,1:T(8,128)S(1)} %get-tuple-element.34), channel_id=1, replica_groups=mesh['expert'=64,'tensor'=4] {'tensor'}, use_global_device_ids=true, to_apply=%region_7.8 | all-reduce | flops 1024 | bytes 8192 | tf_op jit(solution)/shard_map/psum | solution.py:209
  256.3 3.5 %multiply_reduce_fusion = bf16[128,896]{1,0:T(8,128)(2,1)} fusion(bf16[1024,896]{1,0:T(8,128)(2,1)} %gather_fusion, f32[128,8]{1,0:T(8,128)S(1)} %copy.33, pred[128,8]{1,0:T(8,128)(4,1)S(1)} %copy.34), kind=kLoop, calls=%fused_computation.15 | loop fusion | flops 3555328 | bytes 2069504 | tf_op jit(solution)/shard_map/reduce_sum | solution.py:199
  259.8 2.2 convolution_convert_fusion.4
  (39 shorter events, 0.3 us)
Async XLA Ops:
  7.2 91.6 %copy-start = (bf16[1,3584,256]{2,1,0:T(8,128)(2,1)S(1)}, bf16[1,3584,256]{2,1,0:T(8,128)(2,1)}, u32[]{:S(2)}) copy-start(bf16[1,3584,256]{2,1,0:T(8,128)(2,1)} %param.16) | copy-start | bytes 5505028
  11.8 36.3 %all-to-all-start = ((bf16[64,8,896]{2,1,0:T(8,128)(2,1)}), bf16[64,8,896]{2,1,0:T(8,128)(2,1)S(1)}, u32[]{:S(2)}, u32[]{:S(2)}) async-start(bf16[64,8,896]{2,1,0:T(8,128)(2,1)} %fusion.14), calls=%async_computation | async-start | bytes 1835008 | tf_op jit(solution)/shard_map/all_to_all | solution.py:158
  48.2 23.9 %collective-permute-start = (bf16[512,896]{1,0:T(8,128)(2,1)S(1)}, bf16[512,896]{1,0:T(8,128)(2,1)}, u32[]{:S(2)}, u32[]{:S(2)}) collective-permute-start(bf16[512,896]{1,0:T(8,128)(2,1)S(1)} %bitcast.70), channel_id=1, source_target_pairs={{0,1},{1,2},{2,3},{3,0},{4,5},{5,6},{6,7},{7,4},{8,9},{9,10},{10,1... | collective-permute-start | bytes 2752520 | tf_op jit(solution)/shard_map/ppermute | solution.py:26
  49.7 36.3 %collective-permute-start.1 = (bf16[512,896]{1,0:T(8,128)(2,1)S(1)}, bf16[512,896]{1,0:T(8,128)(2,1)}, u32[]{:S(2)}, u32[]{:S(2)}) collective-permute-start(bf16[512,896]{1,0:T(8,128)(2,1)S(1)} %bitcast.71), channel_id=1, source_target_pairs={{0,3},{1,0},{2,1},{3,2},{4,7},{5,4},{6,5},{7,6},{8,11},{9,8},{10,9... | collective-permute-start | bytes 2752520 | tf_op jit(solution)/shard_map/ppermute | solution.py:34
  72.1 24.3 %collective-permute-start.2 = (bf16[512,896]{1,0:T(8,128)(2,1)}, bf16[512,896]{1,0:T(8,128)(2,1)}, u32[]{:S(2)}, u32[]{:S(2)}) collective-permute-start(bf16[512,896]{1,0:T(8,128)(2,1)} %collective-permute-done), channel_id=1, source_target_pairs={{0,1},{1,2},{2,3},{3,0},{4,5},{5,6},{6,7},{7,4},{8,9},{9,10},{10,1... | collective-permute-start | bytes 2752520 | tf_op jit(solution)/shard_map/ppermute | solution.py:26
  76.7 90.1 %all-to-all-start.2 = ((bf16[64,8,3584]{2,1,0:T(8,128)(2,1)}), bf16[64,8,3584]{2,1,0:T(8,128)(2,1)}, u32[]{:S(2)}, u32[]{:S(2)}) async-start(bf16[64,8,3584]{2,1,0:T(8,128)(2,1)} %bitcast.69), calls=%async_computation.3 | async-start | bytes 7340032 | tf_op jit(solution)/shard_map/all_to_all | solution.py:167
  84.2 91.2 %reduce-scatter.3.cloned.1.call-start = ((), (), s32[]{:S(2)}) async-start(), calls=%async_computation.6 | async-start | bytes 4587520 | tf_op jit(solution)/shard_map/reduce_scatter | solution.py:175
  84.5 13.1 %copy-start.4 = (bf16[1,3584,256]{2,1,0:T(8,128)(2,1)S(1)}, bf16[1,3584,256]{2,1,0:T(8,128)(2,1)}, u32[]{:S(2)}) copy-start(bf16[1,3584,256]{2,1,0:T(8,128)(2,1)} %param.15) | copy-start | bytes 5505028
  97.6 3.2 %copy-start.2 = (bf16[512,3584]{1,0:T(8,128)(2,1)}, bf16[512,3584]{1,0:T(8,128)(2,1)S(1)}, u32[]{:S(2)}) copy-start(bf16[512,3584]{1,0:T(8,128)(2,1)S(1)} %constant_dynamic-update-slice_fusion) | copy-start | bytes 11010052
  98.8 2.7 %copy-start.1 = (bf16[256,4,896]{2,1,0:T(4,128)(2,1)S(1)}, bf16[256,4,896]{2,1,0:T(4,128)(2,1)}, u32[]{:S(2)}) copy-start(bf16[256,4,896]{2,1,0:T(4,128)(2,1)} %reshape_squeeze.9) | copy-start | bytes 5505028
  100.8 0.7 copy-start.6
  104.6 114.4 %reduce-scatter.5.cloned.1.call-start = ((), (), s32[]{:S(2)}) async-start(), calls=%async_computation.7 | async-start | bytes 4587520 | tf_op jit(solution)/shard_map/reduce_scatter | solution.py:184
  166.8 3.9 %copy-start.11 = (f32[512,256]{1,0:T(8,128)S(1)}, f32[512,256]{1,0:T(8,128)}, u32[]{:S(2)}) copy-start(f32[512,256]{1,0:T(8,128)} %get-tuple-element.17) | copy-start | bytes 1572868
  166.8 3.9 %copy-start.12 = (f32[512,256]{1,0:T(8,128)S(1)}, f32[512,256]{1,0:T(8,128)}, u32[]{:S(2)}) copy-start(f32[512,256]{1,0:T(8,128)} %get-tuple-element.16) | copy-start | bytes 1572868
  166.8 4.2 %copy-start.5 = (bf16[1,3584,256]{2,1,0:T(8,128)(2,1)S(1)}, bf16[1,3584,256]{2,1,0:T(8,128)(2,1)}, u32[]{:S(2)}) copy-start(bf16[1,3584,256]{2,1,0:T(8,128)(2,1)} %param.15) | copy-start | bytes 5505028
  171.0 1.2 copy-start.7
  171.0 1.2 copy-start.9
  175.4 32.0 %all-to-all-start.1 = ((bf16[64,8,896]{2,1,0:T(8,128)(2,1)}), bf16[64,8,896]{2,1,0:T(8,128)(2,1)S(1)}, u32[]{:S(2)}, u32[]{:S(2)}) async-start(bf16[64,8,896]{2,1,0:T(8,128)(2,1)} %bitcast.75), calls=%async_computation.2 | async-start | bytes 1835008 | tf_op jit(solution)/shard_map/all_to_all | solution.py:177
  218.9 40.9 %all-to-all-start.3 = ((bf16[64,8,896]{2,1,0:T(8,128)(2,1)}), bf16[64,8,896]{2,1,0:T(8,128)(2,1)}, u32[]{:S(2)}, u32[]{:S(2)}) async-start(bf16[64,8,896]{2,1,0:T(8,128)(2,1)} %bitcast.74), calls=%async_computation.5 | async-start | bytes 1835008 | tf_op jit(solution)/shard_map/all_to_all | solution.py:185
  229.8 4.7 %copy-start.3 = (bf16[512,3584]{1,0:T(8,128)(2,1)S(1)}, bf16[512,3584]{1,0:T(8,128)(2,1)}, u32[]{:S(2)}) copy-start(bf16[512,3584]{1,0:T(8,128)(2,1)} %copy-done.2) | copy-start | bytes 11010052
  229.8 4.7 %copy-start.10 = (bf16[512,256]{1,0:T(8,128)(2,1)S(1)}, bf16[512,256]{1,0:T(8,128)(2,1)}, u32[]{:S(2)}) copy-start(bf16[512,256]{1,0:T(8,128)(2,1)} %copy-done.9) | copy-start | bytes 786436
  234.5 2.4 copy-start.8
  239.3 7.7 %copy-start.13 = (f32[128,8]{0,1:T(8,128)S(1)}, f32[128,8]{0,1:T(8,128)}, u32[]{:S(2)}) copy-start(f32[128,8]{0,1:T(8,128)} %param.13) | copy-start | bytes 12292
Sparse Core Ops, SparseCore 0:
  104.7 40.1 reduce-scatter.2
  175.4 43.4 reduce-scatter.4
